TPU v7x, 1024 devices: a whole 4x8x16 slice. The times are simulated.
1024 devices in a mesh: row: 16 (over z), col: 16 (over y_lo, x, core), rep: 4 (over y_hi).
Axes of the slice: x: 4, y: 8 (y_hi: 4, y_lo: 2; y = y_hi * 2 + y_lo), z: 16, core: 2. Of those that a mesh axis runs over, the one named last changes fastest.
Arguments:
- density_blocks: bfloat16 [16, 64, 128, 256], P('row', ('col', 'rep')), may hold values from -0.5 to 0.5
- density_columns: int32 [16, 64, 2], P('row', ('col', 'rep')), may hold values from 0 to 3, as said below
- square_pattern: int32 [16, 64, 2], P('row', ('col', 'rep')), may hold values from 0 to 3
- cube_pattern: int32 [16, 64, 2], P('row', ('col', 'rep')), may hold values from 0 to 3
Outputs:
- purified: float32 [16, 64, 128, 256], P('row', ('col', 'rep'))
Inputs may be any that keep to these rules, and one draw needn't show every extreme that they name: `density_columns`: the 2 block columns of one block row within one tile are all different.
All inputs are finite; a program needn't handle non-finite values.
Results may differ from a plain program's by a relative error of at most 0.0029.
Values may be sent and summed in bfloat16 or wider, within the bound.
No kernel may reach another device: no remote copies, remote signals or barrier semaphores. Data moves between devices by JAX's collectives and lax.ppermute only.
A program may use at most 32 MiB of HBM per device.

v0:
```python
import jax
import jax.numpy as jnp
from jax import lax
from jax.sharding import PartitionSpec as P


def for_sending(x):

    def short(part):
        return part.astype(jnp.bfloat16) if part.dtype == jnp.float32 else part

    return jax.tree.map(short, x)


def passed_along(block, axis, distance):
    devices = range(lax.axis_size(axis))
    route = [((i - distance) % len(devices), i) for i in devices]
    return lax.ppermute(block, axis, route)


def roll_rows(blocks, columns, offset):
    return (
        passed_along(blocks, "row", offset),
        passed_along(for_sending(columns), "row", offset).astype(columns.dtype),
    )


def roll_cols(blocks, columns, offset):
    return (
        passed_along(blocks, "col", offset),
        passed_along(for_sending(columns), "col", offset).astype(columns.dtype),
    )


def gather_layers(blocks, indices):
    return (
        lax.all_gather(blocks, "rep", axis=0, tiled=True),
        lax.all_gather(indices, "rep", axis=0, tiled=True),
    )


def reduce_layers(partial_sum):
    return lax.psum_scatter(partial_sum, "rep", scatter_dimension=0, tiled=True)


def shift_steps(blocks, columns, distance, roller, first_bit, last_bit):
    for bit_index in range(first_bit, last_bit):
        arrived_blocks, arrived_cols = roller(blocks, columns, 1 << bit_index)
        selected = distance >> bit_index & 1 == 1
        blocks = jnp.where(selected, arrived_blocks, blocks)
        columns = jnp.where(selected, arrived_cols, columns)
    return (blocks, columns)


def block_product(left_tile, left_cols, right_tile, right_cols, targets):
    row_count, block_size, left_width = left_tile.shape
    left_slots = left_width // block_size
    right_slots = right_tile.shape[2] // block_size
    target_slots = targets.shape[1]
    picked_rows = jnp.take(right_tile, left_cols, axis=0)
    picked_cols = jnp.take(right_cols, left_cols, axis=0)
    split_right = picked_rows.reshape(row_count, left_slots, block_size, right_slots, block_size)
    matching = (picked_cols[:, :, None, :] == targets[:, None, :, None]).astype(jnp.bfloat16)
    chosen = jnp.einsum(
        "iptq,ipzqy->ipzty", matching, split_right, preferred_element_type=jnp.float32
    ).astype(jnp.bfloat16)
    split_left = left_tile.reshape(row_count, block_size, left_slots, block_size)
    combined = jnp.einsum(
        "ixpz,ipzty->ixty", split_left, chosen, preferred_element_type=jnp.float32
    )
    return combined.reshape(row_count, block_size, target_slots * block_size)


def cannon_sum(left_tile, left_cols, right_tile, right_cols, targets, step_count):
    running = jnp.zeros(
        (left_tile.shape[0], left_tile.shape[1], targets.shape[1] * left_tile.shape[1]), jnp.float32
    )
    for step_index in range(step_count):
        running = running + block_product(left_tile, left_cols, right_tile, right_cols, targets)
        if step_index + 1 < step_count:
            left_tile, left_cols = roll_rows(left_tile, left_cols, -1)
            right_tile, right_cols = roll_cols(right_tile, right_cols, -1)
    return running


def carry_over(second_power, square_pattern, cube_pattern):
    tile_count, row_count, block_size, width = second_power.shape
    slot_count = width // block_size
    matching = (square_pattern[:, :, None, :] == cube_pattern[:, :, :, None]).astype(jnp.float32)
    split_two = second_power.astype(jnp.float32).reshape(
        tile_count, row_count, block_size, slot_count, block_size
    )
    carried = jnp.einsum("jgtu,jgxuy->jgxty", matching, split_two, precision=lax.Precision.HIGHEST)
    return carried.reshape(tile_count, row_count, block_size, cube_pattern.shape[2] * block_size)


def on_device(density_blocks, density_columns, square_pattern, cube_pattern):
    cycle_size = lax.axis_size("row")
    layer_count = lax.axis_size("rep")
    step_count = cycle_size // layer_count
    bit_count = (cycle_size - 1).bit_length()
    row_index = lax.axis_index("row")
    col_index = lax.axis_index("col")
    layer_index = lax.axis_index("rep")
    own_blocks = density_blocks[0]
    own_columns = density_columns[0]
    own_square = square_pattern[0]
    own_cube = cube_pattern[0]
    slot_count = own_columns.shape[1]
    layer_start = layer_index * step_count
    left_distance = (cycle_size - (col_index + layer_start) % cycle_size) % cycle_size
    whole_tile, whole_index = gather_layers(
        own_blocks, jnp.concatenate([own_columns, own_square], axis=1)
    )
    whole_cols = whole_index[:, :slot_count]
    square_targets = whole_index[:, slot_count:]
    right_distance = (cycle_size - (row_index + layer_start) % cycle_size) % cycle_size
    left_tile, left_cols = shift_steps(
        whole_tile, whole_cols, left_distance, roll_rows, 0, bit_count
    )
    right_tile, right_cols = shift_steps(
        whole_tile, whole_cols, right_distance, roll_cols, 0, bit_count
    )
    partial_square = cannon_sum(
        left_tile, left_cols, right_tile, right_cols, square_targets, step_count
    )
    second_power = reduce_layers(partial_square).astype(jnp.bfloat16)
    second_whole, cube_targets = gather_layers(second_power, own_cube)
    second_tile, second_cols = shift_steps(
        second_whole, square_targets, left_distance, roll_rows, 0, bit_count
    )
    partial_cube = cannon_sum(
        second_tile, second_cols, right_tile, right_cols, cube_targets, step_count
    )
    third_power = reduce_layers(partial_cube)
    carried = carry_over(second_power[None], square_pattern, cube_pattern)
    return 3.0 * carried - 2.0 * third_power[None]


def solution(mesh):
    return jax.shard_map(
        on_device,
        mesh=mesh,
        in_specs=(
            P("row", ("col", "rep"), None, None),
            P("row", ("col", "rep"), None),
            P("row", ("col", "rep"), None),
            P("row", ("col", "rep"), None),
        ),
        out_specs=P("row", ("col", "rep"), None, None),
        check_vma=False,
    )
```

profile of v0, /device:TPU:6, one launch (start us, length us, event | category | flops | bytes accessed | tf_op | source)
XLA Modules:
  0.0 464.6 jit_solution(12390312303917830109)
XLA Ops:
  6.5 17.1 %all-gather = bf16[4,1,128,256]{3,2,1,0:T(8,128)(2,1)S(1)} all-gather(bf16[1,1,128,256]{3,2,1,0:T(8,128)(2,1)} %param.8), channel_id=2, replica_groups=mesh['row'=16,'col'=16,'rep'=4] {'rep'}, dimensions={0}, use_global_device_ids=true | all-gather | bytes 327680 | tf_op jit(solution)/shard_map/all_gather | solution.py:37
  26.5 4.3 collective-permute-start
  30.8 9.7 %all-gather.2 = s32[4,1,4]{2,1,0:T(1,128)S(1)} all-gather(s32[1,1,4]{2,1,0:T(1,128)S(1)} %add_bitcast_fusion), channel_id=1, replica_groups=mesh['row'=16,'col'=16,'rep'=4] {'rep'}, dimensions={0}, use_global_device_ids=true | all-gather | bytes 80 | tf_op jit(solution)/shard_map/all_gather | solution.py:38
  42.4 4.3 collective-permute-start.8
  46.7 4.3 collective-permute-start.32
  51.7 10.2 %all-gather.1 = s32[4,1,2]{2,1,0:T(1,128)S(1)} all-gather(s32[1,1,2]{2,1,0:T(1,128)S(1)} %copy-done), channel_id=3, replica_groups=mesh['row'=16,'col'=16,'rep'=4] {'rep'}, dimensions={0}, use_global_device_ids=true | all-gather | bytes 40 | tf_op jit(solution)/shard_map/all_gather | solution.py:38
  62.0 7.3 %collective-permute-start.9 = (s32[4,2]{1,0:T(4,128)S(1)}, s32[4,2]{1,0:T(4,128)S(1)}, u32[]{:S(2)}, u32[]{:S(2)}) collective-permute-start(s32[4,2]{1,0:T(4,128)S(1)} %get-tuple-element.15), channel_id=1, source_target_pairs={{896,0},{960,64},{0,128},{64,192},{128,256},{192,320},{256,384},{3... | collective-permute-start | bytes 104 | tf_op jit(solution)/shard_map/ppermute | solution.py:18
  71.4 6.1 %collective-permute-start.33 = (s32[4,2]{1,0:T(4,128)S(1)}, s32[4,2]{1,0:T(4,128)S(1)}, u32[]{:S(2)}, u32[]{:S(2)}) collective-permute-start(s32[4,2]{1,0:T(4,128)S(1)} %get-tuple-element.13), channel_id=1, source_target_pairs={{896,0},{960,64},{0,128},{64,192},{128,256},{192,320},{256,384},{3... | collective-permute-start | bytes 104 | tf_op jit(solution)/shard_map/ppermute | solution.py:18
  77.5 8.2 %collective-permute-start.10 = (s32[4,2]{1,0:T(4,128)S(1)}, s32[4,2]{1,0:T(4,128)S(1)}, u32[]{:S(2)}, u32[]{:S(2)}) collective-permute-start(s32[4,2]{1,0:T(4,128)S(1)} %broadcast_select_fusion.35), channel_id=1, source_target_pairs={{768,0},{832,64},{896,128},{960,192},{0,256},{64,320},{128,384},{1... | collective-permute-start | bytes 104 | tf_op jit(solution)/shard_map/ppermute | solution.py:18
  85.8 4.3 collective-permute-start.14
  90.1 6.1 %collective-permute-start.34 = (s32[4,2]{1,0:T(4,128)S(1)}, s32[4,2]{1,0:T(4,128)S(1)}, u32[]{:S(2)}, u32[]{:S(2)}) collective-permute-start(s32[4,2]{1,0:T(4,128)S(1)} %broadcast_select_fusion.34), channel_id=1, source_target_pairs={{768,0},{832,64},{896,128},{960,192},{0,256},{64,320},{128,384},{1... | collective-permute-start | bytes 104 | tf_op jit(solution)/shard_map/ppermute | solution.py:18
  96.3 2.7 collective-permute-start.11
  99.0 3.7 collective-permute-start.15
  102.7 11.9 %collective-permute-start.35 = (s32[4,2]{1,0:T(4,128)S(1)}, s32[4,2]{1,0:T(4,128)S(1)}, u32[]{:S(2)}, u32[]{:S(2)}) collective-permute-start(s32[4,2]{1,0:T(4,128)S(1)} %broadcast_select_fusion.36), channel_id=1, source_target_pairs={{512,0},{576,64},{640,128},{704,192},{768,256},{832,320},{896,384}... | collective-permute-start | bytes 104 | tf_op jit(solution)/shard_map/ppermute | solution.py:18
  114.6 3.7 collective-permute-start.18
  118.3 2.5 collective-permute-start.37
  126.3 2.7 collective-permute-start.22
  129.1 2.7 collective-permute-start.23
  131.8 3.4 collective-permute-start.39
  136.1 3.9 collective-permute-start.26
  142.0 6.6 %collective-permute-start.5 = (bf16[4,128,256]{1,2,0:T(8,128)(2,1)S(1)}, bf16[4,128,256]{1,2,0:T(8,128)(2,1)S(1)}, u32[]{:S(2)}, u32[]{:S(2)}) collective-permute-start(bf16[4,128,256]{1,2,0:T(8,128)(2,1)S(1)} %get-tuple-element.11), channel_id=1, source_target_pairs={{56,0},{60,4},{0,8},{4,12},{8,16},{12,20},{16,24},{20,28},{24,32},... | collective-permute-start | bytes 786440 | tf_op jit(solution)/shard_map/ppermute | solution.py:18
  148.7 3.2 collective-permute-start.1
  154.2 4.1 collective-permute-start.6
  158.3 5.3 %collective-permute-done.1 = bf16[4,128,256]{1,2,0:T(8,128)(2,1)S(1)} collective-permute-done((bf16[4,128,256]{1,2,0:T(8,128)(2,1)S(1)}, bf16[4,128,256]{1,2,0:T(8,128)(2,1)S(1)}, u32[]{:S(2)}, u32[]{:S(2)}) %collective-permute-start.1) | collective-permute-done | bytes 262176 | tf_op jit(solution)/shard_map/ppermute | solution.py:18
  163.6 6.8 %collective-permute-start.2 = (bf16[4,128,256]{1,2,0:T(8,128)(2,1)S(1)}, bf16[4,128,256]{1,2,0:T(8,128)(2,1)S(1)}, u32[]{:S(2)}, u32[]{:S(2)}) collective-permute-start(bf16[4,128,256]{1,2,0:T(8,128)(2,1)S(1)} %broadcast_select_fusion.15), channel_id=1, source_target_pairs={{768,0},{832,64},{896,128},{960,192},{0,256},{64,320},{128,384},{1... | collective-permute-start | bytes 786440 | tf_op jit(solution)/shard_map/ppermute | solution.py:18
  173.4 16.4 %collective-permute-done.2 = bf16[4,128,256]{1,2,0:T(8,128)(2,1)S(1)} collective-permute-done((bf16[4,128,256]{1,2,0:T(8,128)(2,1)S(1)}, bf16[4,128,256]{1,2,0:T(8,128)(2,1)S(1)}, u32[]{:S(2)}, u32[]{:S(2)}) %collective-permute-start.2) | collective-permute-done | bytes 262176 | tf_op jit(solution)/shard_map/ppermute | solution.py:18
  189.8 8.6 %collective-permute-start.3 = (bf16[4,128,256]{1,2,0:T(8,128)(2,1)S(1)}, bf16[4,128,256]{1,2,0:T(8,128)(2,1)S(1)}, u32[]{:S(2)}, u32[]{:S(2)}) collective-permute-start(bf16[4,128,256]{1,2,0:T(8,128)(2,1)S(1)} %broadcast_select_fusion.17), channel_id=1, source_target_pairs={{512,0},{576,64},{640,128},{704,192},{768,256},{832,320},{896,384}... | collective-permute-start | bytes 786440 | tf_op jit(solution)/shard_map/ppermute | solution.py:18
  201.2 20.4 %collective-permute-done.3 = bf16[4,128,256]{1,2,0:T(8,128)(2,1)S(1)} collective-permute-done((bf16[4,128,256]{1,2,0:T(8,128)(2,1)S(1)}, bf16[4,128,256]{1,2,0:T(8,128)(2,1)S(1)}, u32[]{:S(2)}, u32[]{:S(2)}) %collective-permute-start.3) | collective-permute-done | bytes 262176 | tf_op jit(solution)/shard_map/ppermute | solution.py:18
  226.8 4.8 %collective-permute-done.16 = bf16[4,128,256]{1,2,0:T(8,128)(2,1)S(1)} collective-permute-done((bf16[4,128,256]{1,2,0:T(8,128)(2,1)S(1)}, bf16[4,128,256]{1,2,0:T(8,128)(2,1)S(1)}, u32[]{:S(2)}, u32[]{:S(2)}) %collective-permute-start.16) | collective-permute-done | bytes 262176 | tf_op jit(solution)/shard_map/ppermute | solution.py:18
  231.9 3.4 collective-permute-start.20
  237.7 3.5 collective-permute-done.21
  242.4 4.1 collective-permute-start.25
  252.3 5.9 %collective-permute-done.24 = bf16[4,128,256]{1,2,0:T(8,128)(2,1)S(1)} collective-permute-done((bf16[4,128,256]{1,2,0:T(8,128)(2,1)S(1)}, bf16[4,128,256]{1,2,0:T(8,128)(2,1)S(1)}, u32[]{:S(2)}, u32[]{:S(2)}) %collective-permute-start.24) | collective-permute-done | bytes 262176 | tf_op jit(solution)/shard_map/ppermute | solution.py:18
  260.6 3.0 collective-permute-start.41
  263.6 2.4 collective-permute-done.41
  266.1 23.5 %reduce-scatter.3.cloned.1.call-done = f32[1,128,256]{2,1,0:T(8,128)} async-done(((f32[4,128,256]{2,1,0:T(8,128)}), f32[1,128,256]{2,1,0:T(8,128)}) %reduce-scatter.3.cloned.1.call-update) | async-done | bytes 131088 | tf_op jit(solution)/shard_map/reduce_scatter | solution.py:43
  290.5 15.0 %all_gather.14 = bf16[4,128,256]{2,1,0:T(8,128)(2,1)S(1)} all-gather(bf16[1,128,256]{2,1,0:T(8,128)(2,1)S(1)} %convert_element_type.69), channel_id=1, replica_groups=mesh['row'=16,'col'=16,'rep'=4] {'rep'}, dimensions={0}, use_global_device_ids=true | all-gather | bytes 327680 | tf_op jit(solution)/shard_map/all_gather | solution.py:37
  305.7 3.3 collective-permute-start.28
  310.5 11.2 %collective-permute-done.28 = bf16[4,128,256]{1,2,0:T(8,128)(2,1)S(1)} collective-permute-done((bf16[4,128,256]{1,2,0:T(8,128)(2,1)S(1)}, bf16[4,128,256]{1,2,0:T(8,128)(2,1)S(1)}, u32[]{:S(2)}, u32[]{:S(2)}) %collective-permute-start.28) | collective-permute-done | bytes 262176 | tf_op jit(solution)/shard_map/ppermute | solution.py:18
  325.6 18.0 %collective-permute-done.29 = bf16[4,128,256]{1,2,0:T(8,128)(2,1)S(1)} collective-permute-done((bf16[4,128,256]{1,2,0:T(8,128)(2,1)S(1)}, bf16[4,128,256]{1,2,0:T(8,128)(2,1)S(1)}, u32[]{:S(2)}, u32[]{:S(2)}) %collective-permute-start.29) | collective-permute-done | bytes 262176 | tf_op jit(solution)/shard_map/ppermute | solution.py:18
  347.8 18.9 %collective-permute-done.30 = bf16[4,128,256]{1,2,0:T(8,128)(2,1)S(1)} collective-permute-done((bf16[4,128,256]{1,2,0:T(8,128)(2,1)S(1)}, bf16[4,128,256]{1,2,0:T(8,128)(2,1)S(1)}, u32[]{:S(2)}, u32[]{:S(2)}) %collective-permute-start.30) | collective-permute-done | bytes 262176 | tf_op jit(solution)/shard_map/ppermute | solution.py:18
  366.8 17.7 %collective-permute-start.31 = (bf16[4,128,256]{1,2,0:T(8,128)(2,1)S(1)}, bf16[4,128,256]{1,2,0:T(8,128)(2,1)S(1)}, u32[]{:S(2)}, u32[]{:S(2)}) collective-permute-start(bf16[4,128,256]{1,2,0:T(8,128)(2,1)S(1)} %broadcast_select_fusion.16), channel_id=1, source_target_pairs={{512,0},{576,64},{640,128},{704,192},{768,256},{832,320},{896,384}... | collective-permute-start | bytes 786440 | tf_op jit(solution)/shard_map/ppermute | solution.py:18
  386.4 4.1 collective-permute-done.31
  393.8 7.7 %collective-permute-done.36 = bf16[4,128,256]{1,2,0:T(8,128)(2,1)S(1)} collective-permute-done((bf16[4,128,256]{1,2,0:T(8,128)(2,1)S(1)}, bf16[4,128,256]{1,2,0:T(8,128)(2,1)S(1)}, u32[]{:S(2)}, u32[]{:S(2)}) %collective-permute-start.36) | collective-permute-done | bytes 262176 | tf_op jit(solution)/shard_map/ppermute | solution.py:18
  404.6 7.4 %collective-permute-done.38 = bf16[4,128,256]{1,2,0:T(8,128)(2,1)S(1)} collective-permute-done((bf16[4,128,256]{1,2,0:T(8,128)(2,1)S(1)}, bf16[4,128,256]{1,2,0:T(8,128)(2,1)S(1)}, u32[]{:S(2)}, u32[]{:S(2)}) %collective-permute-start.38) | collective-permute-done | bytes 262176 | tf_op jit(solution)/shard_map/ppermute | solution.py:18
  412.0 3.8 collective-permute-start.40
  416.2 4.1 collective-permute-done.40
  422.1 34.1 %reduce-scatter.5.cloned.1.call-done = f32[1,128,256]{2,1,0:T(8,128)} async-done(((f32[4,128,256]{2,1,0:T(8,128)}), f32[1,128,256]{2,1,0:T(8,128)}) %reduce-scatter.5.cloned.1.call-update) | async-done | bytes 131088 | tf_op jit(solution)/shard_map/reduce_scatter | solution.py:43
  (186 shorter events, 63.6 us)
Async XLA Ops:
  6.5 283.1 %reduce-scatter.3.cloned.1.call-start = ((), (), s32[]{:S(2)}) async-start(), calls=%async_computation.2 | async-start | bytes 655360 | tf_op jit(solution)/shard_map/reduce_scatter | solution.py:43
  23.8 118.2 %collective-permute-start.4 = (bf16[4,128,256]{1,2,0:T(8,128)(2,1)S(1)}, bf16[4,128,256]{1,2,0:T(8,128)(2,1)S(1)}, u32[]{:S(2)}, u32[]{:S(2)}) collective-permute-start(bf16[4,128,256]{1,2,0:T(8,128)(2,1)S(1)} %bitcast.215), channel_id=1, source_target_pairs={{60,0},{0,4},{4,8},{8,12},{12,16},{16,20},{20,24},{24,28},{28,32},... | collective-permute-start | bytes 786440 | tf_op jit(solution)/shard_map/ppermute | solution.py:18
  25.7 0.7 copy-start.1
  25.7 0.7 copy-start.2
  26.5 115.5 %collective-permute-start = (bf16[4,128,256]{1,2,0:T(8,128)(2,1)S(1)}, bf16[4,128,256]{1,2,0:T(8,128)(2,1)S(1)}, u32[]{:S(2)}, u32[]{:S(2)}) collective-permute-start(bf16[4,128,256]{1,2,0:T(8,128)(2,1)S(1)} %bitcast.216), channel_id=1, source_target_pairs={{960,0},{0,64},{64,128},{128,192},{192,256},{256,320},{320,384},{3... | collective-permute-start | bytes 786440 | tf_op jit(solution)/shard_map/ppermute | solution.py:18
  40.5 21.4 %collective-permute-start.12 = (s32[4,2]{1,0:T(4,128)S(1)}, s32[4,2]{1,0:T(4,128)S(1)}, u32[]{:S(2)}, u32[]{:S(2)}) collective-permute-start(s32[4,2]{1,0:T(4,128)S(1)} %get-tuple-element.17), channel_id=1, source_target_pairs={{60,0},{0,4},{4,8},{8,12},{12,16},{16,20},{20,24},{24,28},{28,32},... | collective-permute-start | bytes 104 | tf_op jit(solution)/shard_map/ppermute | solution.py:18
  42.4 19.5 %collective-permute-start.8 = (s32[4,2]{1,0:T(4,128)S(1)}, s32[4,2]{1,0:T(4,128)S(1)}, u32[]{:S(2)}, u32[]{:S(2)}) collective-permute-start(s32[4,2]{1,0:T(4,128)S(1)} %get-tuple-element.17), channel_id=1, source_target_pairs={{960,0},{0,64},{64,128},{128,192},{192,256},{256,320},{320,384},{3... | collective-permute-start | bytes 104 | tf_op jit(solution)/shard_map/ppermute | solution.py:18
  46.7 15.2 %collective-permute-start.32 = (s32[4,2]{1,0:T(4,128)S(1)}, s32[4,2]{1,0:T(4,128)S(1)}, u32[]{:S(2)}, u32[]{:S(2)}) collective-permute-start(s32[4,2]{1,0:T(4,128)S(1)} %get-tuple-element.16), channel_id=1, source_target_pairs={{960,0},{0,64},{64,128},{128,192},{192,256},{256,320},{320,384},{3... | collective-permute-start | bytes 104 | tf_op jit(solution)/shard_map/ppermute | solution.py:18
  51.1 0.7 copy-start
  62.0 15.5 %collective-permute-start.9 = (s32[4,2]{1,0:T(4,128)S(1)}, s32[4,2]{1,0:T(4,128)S(1)}, u32[]{:S(2)}, u32[]{:S(2)}) collective-permute-start(s32[4,2]{1,0:T(4,128)S(1)} %get-tuple-element.15), channel_id=1, source_target_pairs={{896,0},{960,64},{0,128},{64,192},{128,256},{192,320},{256,384},{3... | collective-permute-start | bytes 104 | tf_op jit(solution)/shard_map/ppermute | solution.py:18
  69.3 16.4 %collective-permute-start.13 = (s32[4,2]{1,0:T(4,128)S(1)}, s32[4,2]{1,0:T(4,128)S(1)}, u32[]{:S(2)}, u32[]{:S(2)}) collective-permute-start(s32[4,2]{1,0:T(4,128)S(1)} %get-tuple-element.14), channel_id=1, source_target_pairs={{56,0},{60,4},{0,8},{4,12},{8,16},{12,20},{16,24},{20,28},{24,32},... | collective-permute-start | bytes 104 | tf_op jit(solution)/shard_map/ppermute | solution.py:18
  71.4 18.7 %collective-permute-start.33 = (s32[4,2]{1,0:T(4,128)S(1)}, s32[4,2]{1,0:T(4,128)S(1)}, u32[]{:S(2)}, u32[]{:S(2)}) collective-permute-start(s32[4,2]{1,0:T(4,128)S(1)} %get-tuple-element.13), channel_id=1, source_target_pairs={{896,0},{960,64},{0,128},{64,192},{128,256},{192,320},{256,384},{3... | collective-permute-start | bytes 104 | tf_op jit(solution)/shard_map/ppermute | solution.py:18
  77.5 18.7 %collective-permute-start.10 = (s32[4,2]{1,0:T(4,128)S(1)}, s32[4,2]{1,0:T(4,128)S(1)}, u32[]{:S(2)}, u32[]{:S(2)}) collective-permute-start(s32[4,2]{1,0:T(4,128)S(1)} %broadcast_select_fusion.35), channel_id=1, source_target_pairs={{768,0},{832,64},{896,128},{960,192},{0,256},{64,320},{128,384},{1... | collective-permute-start | bytes 104 | tf_op jit(solution)/shard_map/ppermute | solution.py:18
  85.8 13.2 %collective-permute-start.14 = (s32[4,2]{1,0:T(4,128)S(1)}, s32[4,2]{1,0:T(4,128)S(1)}, u32[]{:S(2)}, u32[]{:S(2)}) collective-permute-start(s32[4,2]{1,0:T(4,128)S(1)} %broadcast_select_fusion.29), channel_id=1, source_target_pairs={{48,0},{52,4},{56,8},{60,12},{0,16},{4,20},{8,24},{12,28},{16,32},... | collective-permute-start | bytes 104 | tf_op jit(solution)/shard_map/ppermute | solution.py:18
  90.1 12.6 %collective-permute-start.34 = (s32[4,2]{1,0:T(4,128)S(1)}, s32[4,2]{1,0:T(4,128)S(1)}, u32[]{:S(2)}, u32[]{:S(2)}) collective-permute-start(s32[4,2]{1,0:T(4,128)S(1)} %broadcast_select_fusion.34), channel_id=1, source_target_pairs={{768,0},{832,64},{896,128},{960,192},{0,256},{64,320},{128,384},{1... | collective-permute-start | bytes 104 | tf_op jit(solution)/shard_map/ppermute | solution.py:18
  96.3 18.3 %collective-permute-start.11 = (s32[4,2]{1,0:T(4,128)S(1)}, s32[4,2]{1,0:T(4,128)S(1)}, u32[]{:S(2)}, u32[]{:S(2)}) collective-permute-start(s32[4,2]{1,0:T(4,128)S(1)} %broadcast_select_fusion.37), channel_id=1, source_target_pairs={{512,0},{576,64},{640,128},{704,192},{768,256},{832,320},{896,384}... | collective-permute-start | bytes 104 | tf_op jit(solution)/shard_map/ppermute | solution.py:18
  99.0 21.8 %collective-permute-start.15 = (s32[4,2]{1,0:T(4,128)S(1)}, s32[4,2]{1,0:T(4,128)S(1)}, u32[]{:S(2)}, u32[]{:S(2)}) collective-permute-start(s32[4,2]{1,0:T(4,128)S(1)} %broadcast_select_fusion.30), channel_id=1, source_target_pairs={{32,0},{36,4},{40,8},{44,12},{48,16},{52,20},{56,24},{60,28},{0,32... | collective-permute-start | bytes 104 | tf_op jit(solution)/shard_map/ppermute | solution.py:18
  102.7 15.6 %collective-permute-start.35 = (s32[4,2]{1,0:T(4,128)S(1)}, s32[4,2]{1,0:T(4,128)S(1)}, u32[]{:S(2)}, u32[]{:S(2)}) collective-permute-start(s32[4,2]{1,0:T(4,128)S(1)} %broadcast_select_fusion.36), channel_id=1, source_target_pairs={{512,0},{576,64},{640,128},{704,192},{768,256},{832,320},{896,384}... | collective-permute-start | bytes 104 | tf_op jit(solution)/shard_map/ppermute | solution.py:18
  114.6 9.9 %collective-permute-start.18 = (s32[4,2]{1,0:T(4,128)S(1)}, s32[4,2]{1,0:T(4,128)S(1)}, u32[]{:S(2)}, u32[]{:S(2)}) collective-permute-start(s32[4,2]{1,0:T(4,128)S(1)} %get-tuple-element.10), channel_id=1, source_target_pairs={{64,0},{128,64},{192,128},{256,192},{320,256},{384,320},{448,384},... | collective-permute-start | bytes 104 | tf_op jit(solution)/shard_map/ppermute | solution.py:18
  118.3 7.1 %collective-permute-start.37 = (s32[4,2]{1,0:T(4,128)S(1)}, s32[4,2]{1,0:T(4,128)S(1)}, u32[]{:S(2)}, u32[]{:S(2)}) collective-permute-start(s32[4,2]{1,0:T(4,128)S(1)} %get-tuple-element.8), channel_id=1, source_target_pairs={{64,0},{128,64},{192,128},{256,192},{320,256},{384,320},{448,384},... | collective-permute-start | bytes 104 | tf_op jit(solution)/shard_map/ppermute | solution.py:18
  120.8 3.8 collective-permute-start.19
  126.3 8.9 %collective-permute-start.22 = (s32[4,2]{1,0:T(4,128)S(1)}, s32[4,2]{1,0:T(4,128)S(1)}, u32[]{:S(2)}, u32[]{:S(2)}) collective-permute-start(s32[4,2]{1,0:T(4,128)S(1)} %collective-permute-done.18), channel_id=1, source_target_pairs={{64,0},{128,64},{192,128},{256,192},{320,256},{384,320},{448,384},... | collective-permute-start | bytes 104 | tf_op jit(solution)/shard_map/ppermute | solution.py:18
  129.1 6.3 %collective-permute-start.23 = (s32[4,2]{1,0:T(4,128)S(1)}, s32[4,2]{1,0:T(4,128)S(1)}, u32[]{:S(2)}, u32[]{:S(2)}) collective-permute-start(s32[4,2]{1,0:T(4,128)S(1)} %collective-permute-done.19), channel_id=1, source_target_pairs={{4,0},{8,4},{12,8},{16,12},{20,16},{24,20},{28,24},{32,28},{36,32}... | collective-permute-start | bytes 104 | tf_op jit(solution)/shard_map/ppermute | solution.py:18
  131.8 127.9 %collective-permute-start.39 = (s32[4,2]{1,0:T(4,128)S(1)}, s32[4,2]{1,0:T(4,128)S(1)}, u32[]{:S(2)}, u32[]{:S(2)}) collective-permute-start(s32[4,2]{1,0:T(4,128)S(1)} %collective-permute-done.37), channel_id=1, source_target_pairs={{64,0},{128,64},{192,128},{256,192},{320,256},{384,320},{448,384},... | collective-permute-start | bytes 104 | tf_op jit(solution)/shard_map/ppermute | solution.py:18
  136.1 12.5 %collective-permute-start.26 = (s32[4,2]{1,0:T(4,128)S(1)}, s32[4,2]{1,0:T(4,128)S(1)}, u32[]{:S(2)}, u32[]{:S(2)}) collective-permute-start(s32[4,2]{1,0:T(4,128)S(1)} %collective-permute-done.22), channel_id=1, source_target_pairs={{64,0},{128,64},{192,128},{256,192},{320,256},{384,320},{448,384},... | collective-permute-start | bytes 104 | tf_op jit(solution)/shard_map/ppermute | solution.py:18
  140.0 30.4 %collective-permute-start.27 = (s32[4,2]{1,0:T(4,128)S(1)}, s32[4,2]{1,0:T(4,128)S(1)}, u32[]{:S(2)}, u32[]{:S(2)}) collective-permute-start(s32[4,2]{1,0:T(4,128)S(1)} %collective-permute-done.23), channel_id=1, source_target_pairs={{4,0},{8,4},{12,8},{16,12},{20,16},{24,20},{28,24},{32,28},{36,32}... | collective-permute-start | bytes 104 | tf_op jit(solution)/shard_map/ppermute | solution.py:18
  142.0 12.1 %collective-permute-start.5 = (bf16[4,128,256]{1,2,0:T(8,128)(2,1)S(1)}, bf16[4,128,256]{1,2,0:T(8,128)(2,1)S(1)}, u32[]{:S(2)}, u32[]{:S(2)}) collective-permute-start(bf16[4,128,256]{1,2,0:T(8,128)(2,1)S(1)} %get-tuple-element.11), channel_id=1, source_target_pairs={{56,0},{60,4},{0,8},{4,12},{8,16},{12,20},{16,24},{20,28},{24,32},... | collective-permute-start | bytes 786440 | tf_op jit(solution)/shard_map/ppermute | solution.py:18
  148.7 14.9 %collective-permute-start.1 = (bf16[4,128,256]{1,2,0:T(8,128)(2,1)S(1)}, bf16[4,128,256]{1,2,0:T(8,128)(2,1)S(1)}, u32[]{:S(2)}, u32[]{:S(2)}) collective-permute-start(bf16[4,128,256]{1,2,0:T(8,128)(2,1)S(1)} %get-tuple-element.12), channel_id=1, source_target_pairs={{896,0},{960,64},{0,128},{64,192},{128,256},{192,320},{256,384},{3... | collective-permute-start | bytes 786440 | tf_op jit(solution)/shard_map/ppermute | solution.py:18
  154.2 17.0 %collective-permute-start.6 = (bf16[4,128,256]{1,2,0:T(8,128)(2,1)S(1)}, bf16[4,128,256]{1,2,0:T(8,128)(2,1)S(1)}, u32[]{:S(2)}, u32[]{:S(2)}) collective-permute-start(bf16[4,128,256]{1,2,0:T(8,128)(2,1)S(1)} %broadcast_select_fusion.9), channel_id=1, source_target_pairs={{48,0},{52,4},{56,8},{60,12},{0,16},{4,20},{8,24},{12,28},{16,32},... | collective-permute-start | bytes 786440 | tf_op jit(solution)/shard_map/ppermute | solution.py:18
  163.6 26.2 %collective-permute-start.2 = (bf16[4,128,256]{1,2,0:T(8,128)(2,1)S(1)}, bf16[4,128,256]{1,2,0:T(8,128)(2,1)S(1)}, u32[]{:S(2)}, u32[]{:S(2)}) collective-permute-start(bf16[4,128,256]{1,2,0:T(8,128)(2,1)S(1)} %broadcast_select_fusion.15), channel_id=1, source_target_pairs={{768,0},{832,64},{896,128},{960,192},{0,256},{64,320},{128,384},{1... | collective-permute-start | bytes 786440 | tf_op jit(solution)/shard_map/ppermute | solution.py:18
  171.2 27.4 %collective-permute-start.7 = (bf16[4,128,256]{1,2,0:T(8,128)(2,1)S(1)}, bf16[4,128,256]{1,2,0:T(8,128)(2,1)S(1)}, u32[]{:S(2)}, u32[]{:S(2)}) collective-permute-start(bf16[4,128,256]{1,2,0:T(8,128)(2,1)S(1)} %broadcast_select_fusion.10), channel_id=1, source_target_pairs={{32,0},{36,4},{40,8},{44,12},{48,16},{52,20},{56,24},{60,28},{0,32... | collective-permute-start | bytes 786440 | tf_op jit(solution)/shard_map/ppermute | solution.py:18
  189.8 31.7 %collective-permute-start.3 = (bf16[4,128,256]{1,2,0:T(8,128)(2,1)S(1)}, bf16[4,128,256]{1,2,0:T(8,128)(2,1)S(1)}, u32[]{:S(2)}, u32[]{:S(2)}) collective-permute-start(bf16[4,128,256]{1,2,0:T(8,128)(2,1)S(1)} %broadcast_select_fusion.17), channel_id=1, source_target_pairs={{512,0},{576,64},{640,128},{704,192},{768,256},{832,320},{896,384}... | collective-permute-start | bytes 786440 | tf_op jit(solution)/shard_map/ppermute | solution.py:18
  198.6 26.2 %collective-permute-start.17 = (bf16[4,128,256]{1,2,0:T(8,128)(2,1)S(1)}, bf16[4,128,256]{1,2,0:T(8,128)(2,1)S(1)}, u32[]{:S(2)}, u32[]{:S(2)}) collective-permute-start(bf16[4,128,256]{1,2,0:T(8,128)(2,1)S(1)} %broadcast_select_fusion.11), channel_id=1, source_target_pairs={{4,0},{8,4},{12,8},{16,12},{20,16},{24,20},{28,24},{32,28},{36,32}... | collective-permute-start | bytes 786440 | tf_op jit(solution)/shard_map/ppermute | solution.py:18
  221.6 10.0 %collective-permute-start.16 = (bf16[4,128,256]{1,2,0:T(8,128)(2,1)S(1)}, bf16[4,128,256]{1,2,0:T(8,128)(2,1)S(1)}, u32[]{:S(2)}, u32[]{:S(2)}) collective-permute-start(bf16[4,128,256]{1,2,0:T(8,128)(2,1)S(1)} %broadcast_select_fusion.19), channel_id=1, source_target_pairs={{64,0},{128,64},{192,128},{256,192},{320,256},{384,320},{448,384},... | collective-permute-start | bytes 786440 | tf_op jit(solution)/shard_map/ppermute | solution.py:18
  231.9 15.3 %collective-permute-start.20 = (bf16[4,128,256]{1,2,0:T(8,128)(2,1)S(1)}, bf16[4,128,256]{1,2,0:T(8,128)(2,1)S(1)}, u32[]{:S(2)}, u32[]{:S(2)}) collective-permute-start(bf16[4,128,256]{1,2,0:T(8,128)(2,1)S(1)} %collective-permute-done.16), channel_id=1, source_target_pairs={{64,0},{128,64},{192,128},{256,192},{320,256},{384,320},{448,384},... | collective-permute-start | bytes 786440 | tf_op jit(solution)/shard_map/ppermute | solution.py:18
  235.4 5.8 %collective-permute-start.21 = (bf16[4,128,256]{1,2,0:T(8,128)(2,1)S(1)}, bf16[4,128,256]{1,2,0:T(8,128)(2,1)S(1)}, u32[]{:S(2)}, u32[]{:S(2)}) collective-permute-start(bf16[4,128,256]{1,2,0:T(8,128)(2,1)S(1)} %collective-permute-done.17), channel_id=1, source_target_pairs={{4,0},{8,4},{12,8},{16,12},{20,16},{24,20},{28,24},{32,28},{36,32}... | collective-permute-start | bytes 786440 | tf_op jit(solution)/shard_map/ppermute | solution.py:18
  242.4 8.0 %collective-permute-start.25 = (bf16[4,128,256]{1,2,0:T(8,128)(2,1)S(1)}, bf16[4,128,256]{1,2,0:T(8,128)(2,1)S(1)}, u32[]{:S(2)}, u32[]{:S(2)}) collective-permute-start(bf16[4,128,256]{1,2,0:T(8,128)(2,1)S(1)} %collective-permute-done.21), channel_id=1, source_target_pairs={{4,0},{8,4},{12,8},{16,12},{20,16},{24,20},{28,24},{32,28},{36,32}... | collective-permute-start | bytes 786440 | tf_op jit(solution)/shard_map/ppermute | solution.py:18
  247.3 11.0 %collective-permute-start.24 = (bf16[4,128,256]{1,2,0:T(8,128)(2,1)S(1)}, bf16[4,128,256]{1,2,0:T(8,128)(2,1)S(1)}, u32[]{:S(2)}, u32[]{:S(2)}) collective-permute-start(bf16[4,128,256]{1,2,0:T(8,128)(2,1)S(1)} %collective-permute-done.20), channel_id=1, source_target_pairs={{64,0},{128,64},{192,128},{256,192},{320,256},{384,320},{448,384},... | collective-permute-start | bytes 786440 | tf_op jit(solution)/shard_map/ppermute | solution.py:18
  259.6 196.6 %reduce-scatter.5.cloned.1.call-start = ((), (), s32[]{:S(2)}) async-start(), calls=%async_computation.3 | async-start | bytes 655360 | tf_op jit(solution)/shard_map/reduce_scatter | solution.py:43
  260.6 5.5 %collective-permute-start.41 = (s32[4,2]{1,0:T(4,128)S(1)}, s32[4,2]{1,0:T(4,128)S(1)}, u32[]{:S(2)}, u32[]{:S(2)}) collective-permute-start(s32[4,2]{1,0:T(4,128)S(1)} %collective-permute-done.39), channel_id=1, source_target_pairs={{64,0},{128,64},{192,128},{256,192},{320,256},{384,320},{448,384},... | collective-permute-start | bytes 104 | tf_op jit(solution)/shard_map/ppermute | solution.py:18
  305.7 16.0 %collective-permute-start.28 = (bf16[4,128,256]{1,2,0:T(8,128)(2,1)S(1)}, bf16[4,128,256]{1,2,0:T(8,128)(2,1)S(1)}, u32[]{:S(2)}, u32[]{:S(2)}) collective-permute-start(bf16[4,128,256]{1,2,0:T(8,128)(2,1)S(1)} %copy.78), channel_id=1, source_target_pairs={{960,0},{0,64},{64,128},{128,192},{192,256},{256,320},{320,384},{3... | collective-permute-start | bytes 786440 | tf_op jit(solution)/shard_map/ppermute | solution.py:18
  321.7 21.9 %collective-permute-start.29 = (bf16[4,128,256]{1,2,0:T(8,128)(2,1)S(1)}, bf16[4,128,256]{1,2,0:T(8,128)(2,1)S(1)}, u32[]{:S(2)}, u32[]{:S(2)}) collective-permute-start(bf16[4,128,256]{1,2,0:T(8,128)(2,1)S(1)} %broadcast_select_fusion.12), channel_id=1, source_target_pairs={{896,0},{960,64},{0,128},{64,192},{128,256},{192,320},{256,384},{3... | collective-permute-start | bytes 786440 | tf_op jit(solution)/shard_map/ppermute | solution.py:18
  343.7 23.0 %collective-permute-start.30 = (bf16[4,128,256]{1,2,0:T(8,128)(2,1)S(1)}, bf16[4,128,256]{1,2,0:T(8,128)(2,1)S(1)}, u32[]{:S(2)}, u32[]{:S(2)}) collective-permute-start(bf16[4,128,256]{1,2,0:T(8,128)(2,1)S(1)} %broadcast_select_fusion.14), channel_id=1, source_target_pairs={{768,0},{832,64},{896,128},{960,192},{0,256},{64,320},{128,384},{1... | collective-permute-start | bytes 786440 | tf_op jit(solution)/shard_map/ppermute | solution.py:18
  366.8 23.7 %collective-permute-start.31 = (bf16[4,128,256]{1,2,0:T(8,128)(2,1)S(1)}, bf16[4,128,256]{1,2,0:T(8,128)(2,1)S(1)}, u32[]{:S(2)}, u32[]{:S(2)}) collective-permute-start(bf16[4,128,256]{1,2,0:T(8,128)(2,1)S(1)} %broadcast_select_fusion.16), channel_id=1, source_target_pairs={{512,0},{576,64},{640,128},{704,192},{768,256},{832,320},{896,384}... | collective-permute-start | bytes 786440 | tf_op jit(solution)/shard_map/ppermute | solution.py:18
  390.5 10.9 %collective-permute-start.36 = (bf16[4,128,256]{1,2,0:T(8,128)(2,1)S(1)}, bf16[4,128,256]{1,2,0:T(8,128)(2,1)S(1)}, u32[]{:S(2)}, u32[]{:S(2)}) collective-permute-start(bf16[4,128,256]{1,2,0:T(8,128)(2,1)S(1)} %broadcast_select_fusion.18), channel_id=1, source_target_pairs={{64,0},{128,64},{192,128},{256,192},{320,256},{384,320},{448,384},... | collective-permute-start | bytes 786440 | tf_op jit(solution)/shard_map/ppermute | solution.py:18
  401.8 10.2 %collective-permute-start.38 = (bf16[4,128,256]{1,2,0:T(8,128)(2,1)S(1)}, bf16[4,128,256]{1,2,0:T(8,128)(2,1)S(1)}, u32[]{:S(2)}, u32[]{:S(2)}) collective-permute-start(bf16[4,128,256]{1,2,0:T(8,128)(2,1)S(1)} %collective-permute-done.36), channel_id=1, source_target_pairs={{64,0},{128,64},{192,128},{256,192},{320,256},{384,320},{448,384},... | collective-permute-start | bytes 786440 | tf_op jit(solution)/shard_map/ppermute | solution.py:18
  412.0 8.3 %collective-permute-start.40 = (bf16[4,128,256]{1,2,0:T(8,128)(2,1)S(1)}, bf16[4,128,256]{1,2,0:T(8,128)(2,1)S(1)}, u32[]{:S(2)}, u32[]{:S(2)}) collective-permute-start(bf16[4,128,256]{1,2,0:T(8,128)(2,1)S(1)} %collective-permute-done.38), channel_id=1, source_target_pairs={{64,0},{128,64},{192,128},{256,192},{320,256},{384,320},{448,384},... | collective-permute-start | bytes 786440 | tf_op jit(solution)/shard_map/ppermute | solution.py:18
Sparse Core Ops, SparseCore 0:
  259.7 29.8 reduce-scatter.2
  421.8 34.3 reduce-scatter.4
where the time goes:
time: 466 us; the launch traced here: 465 us
  waiting for transfers between devices  191 us (41%)
  starting transfers between devices  175 us (38%)
  blocking collectives  52 us (11%)
  local copies, waits for them, and re-layouts  19.3 us (4%)
  between operations  14.5 us (3%)
  matrix products  9.11 us (2%)
    ppermute x42, starting transfers between devices, passed_along(): return lax.ppermute(block, axis, route)  175 us
    ppermute x42, waiting for transfers between devices, passed_along(): return lax.ppermute(block, axis, route)  133 us
    reduce_scatter x2, waiting for transfers between devices, reduce_layers(): return lax.psum_scatter(partial_sum, 'rep', scatter_dimension=0, tiled=True)  57.6 us
    all_gather x2, blocking collectives, gather_layers(): lax.all_gather(blocks, 'rep', axis=0, tiled=True)  32.1 us
    all_gather x2, blocking collectives, gather_layers(): lax.all_gather(indices, 'rep', axis=0, tiled=True)  19.9 us
  transfers between devices with their start and end apart: 44, of which 18 were waited for; matrix products, arithmetic and copies ran while one was open for 6% of the time, Pallas kernels for 0%

commit v1 on v0

v1 whole, which is shorter than its diff:
```python
import jax
import jax.numpy as jnp
from jax import lax
from jax.sharding import PartitionSpec as P

BLOCK = 128
INDEX_ROWS = 16


def with_indices(blocks, indices):
    rows, width = blocks.shape
    tail = jnp.zeros((INDEX_ROWS, width), jnp.bfloat16)
    tail = tail.at[0, : indices.shape[0]].set(indices.astype(jnp.bfloat16))
    return jnp.concatenate([blocks.astype(jnp.bfloat16), tail], axis=0)


def split_indices(gathered, slot_count):
    blocks = gathered[:, :BLOCK, :]
    indices = gathered[:, BLOCK, :slot_count].astype(jnp.int32)
    return blocks, indices


def dense_row(blocks, columns, tile_width):
    tiles, rows, width = blocks.shape
    slots = width // BLOCK
    pieces = blocks.reshape(tiles, rows, slots, BLOCK).astype(jnp.float32)
    total = None
    for p in range(slots):
        hit = columns[:, p][:, None] == jnp.arange(tile_width, dtype=jnp.int32)[None, :]
        term = jnp.where(hit[:, None, :, None], pieces[:, :, p, None, :], 0.0)
        total = term if total is None else total + term
    dense = jnp.transpose(total, (1, 0, 2, 3))
    return dense.reshape(rows, tiles * tile_width * BLOCK).astype(jnp.bfloat16)


def selected_columns(blocks, columns, targets):
    rows_k, rows, width = blocks.shape
    slots = width // BLOCK
    pieces = blocks.reshape(rows_k, rows, slots, BLOCK)
    outs = []
    for q in range(targets.shape[0]):
        chosen = jnp.zeros((rows_k, rows, BLOCK), jnp.bfloat16)
        for p in range(slots):
            hit = columns[:, p] == targets[q]
            chosen = jnp.where(hit[:, None, None], pieces[:, :, p, :], chosen)
        outs.append(chosen)
    stacked = jnp.stack(outs, axis=2)
    return stacked.reshape(rows_k * rows, targets.shape[0] * BLOCK)


def on_device(density_blocks, density_columns, square_pattern, cube_pattern):
    tile_width = 4
    own_blocks = density_blocks[0, 0]
    own_columns = density_columns[0, 0]
    own_square = square_pattern[0, 0]
    own_cube = cube_pattern[0, 0]
    slot_count = own_columns.shape[0]

    payload = with_indices(own_blocks, own_columns)
    row_all = lax.all_gather(payload, "row", axis=0, tiled=False)
    col_all = lax.all_gather(payload, ("col", "rep"), axis=0, tiled=False)
    row_blocks, row_cols = split_indices(row_all, slot_count)
    col_blocks, col_cols = split_indices(col_all, slot_count)

    left = dense_row(row_blocks, row_cols, tile_width)
    right_square = selected_columns(col_blocks, col_cols, own_square)
    square = jnp.dot(left, right_square, preferred_element_type=jnp.float32)
    second_power = square.astype(jnp.bfloat16)

    second_payload = with_indices(second_power, own_square)
    second_all = lax.all_gather(second_payload, "row", axis=0, tiled=False)
    second_blocks, second_cols = split_indices(second_all, slot_count)
    left_two = dense_row(second_blocks, second_cols, tile_width)
    right_cube = selected_columns(col_blocks, col_cols, own_cube)
    third_power = jnp.dot(left_two, right_cube, preferred_element_type=jnp.float32)

    split_two = second_power.astype(jnp.float32).reshape(BLOCK, slot_count, BLOCK)
    carried = []
    for t in range(own_cube.shape[0]):
        acc = jnp.zeros((BLOCK, BLOCK), jnp.float32)
        for u in range(slot_count):
            acc = acc + jnp.where(own_square[u] == own_cube[t], split_two[:, u, :], 0.0)
        carried.append(acc)
    carried = jnp.stack(carried, axis=1).reshape(BLOCK, own_cube.shape[0] * BLOCK)
    purified = 3.0 * carried - 2.0 * third_power
    return purified[None, None]


def solution(mesh):
    return jax.shard_map(
        on_device,
        mesh=mesh,
        in_specs=(
            P("row", ("col", "rep"), None, None),
            P("row", ("col", "rep"), None),
            P("row", ("col", "rep"), None),
            P("row", ("col", "rep"), None),
        ),
        out_specs=P("row", ("col", "rep"), None, None),
        check_vma=False,
    )
```

time: 466 us -> 451 us (0.968)
  starting transfers between devices: 175 us -> 0.08 us
  waiting for transfers between devices: 191 us -> 333 us
  other arithmetic: 4.18 us -> 57.5 us
  blocking collectives: 52 us -> 0 us
  local copies, waits for them, and re-layouts: 19.3 us -> 35.4 us
    all_gather x0 -> x3, waiting for transfers between devices: none -> 332 us  [the longest x1 175 us: on_device(): col_all = lax.all_gather(payload, ('col', 'rep'), axis=0, tiled=False)]
    ppermute x42 -> x0, starting transfers between devices: 175 us -> none  [passed_along(): return lax.ppermute(block, axis, route)]
    ppermute x42 -> x0, waiting for transfers between devices: 133 us -> none  [passed_along(): return lax.ppermute(block, axis, route)]
    reduce_scatter x2 -> x0, waiting for transfers between devices: 57.6 us -> none  [reduce_layers(): return lax.psum_scatter(partial_sum, 'rep', scatter_dimension=0, tiled=True)]
    all_gather x4 -> x0, blocking collectives: 52 us -> none  [the longest x2 32.1 us: gather_layers(): lax.all_gather(blocks, 'rep', axis=0, tiled=True)]
    another operation x0 -> x1, other arithmetic: none -> 20 us  [selected_columns(): stacked = jnp.stack(outs, axis=2)]
    select_n x43 -> x1, other arithmetic: 1.49 us -> 20.9 us  [selected_columns(): chosen = jnp.where(hit[:, None, None], pieces[:, :, p, :], chosen)]
    slice x1 -> x8, local copies, waits for them, and re-layouts: 0.07 us -> 14.3 us  [the longest x1 4.72 us: split_indices(): blocks = gathered[:, :BLOCK, :]]
  transfers between devices with their start and end apart: 44 -> 3, of which waited for: 18 -> 3; matrix products, arithmetic and copies ran while one was open for 6% -> 4% of each run, Pallas kernels for 0% -> 0%
where the time goes in v1:
time: 451 us; the launch traced here: 450 us
  waiting for transfers between devices  333 us (74%)
  other arithmetic  57.5 us (13%)
  local copies, waits for them, and re-layouts  35.4 us (8%)
  between operations  18.6 us (4%)
  matrix products  4.91 us (1%)
    all_gather x1, waiting for transfers between devices, on_device(): col_all = lax.all_gather(payload, ('col', 'rep'), axis=0, tiled=False)  175 us
    all_gather x1, waiting for transfers between devices, on_device(): row_all = lax.all_gather(payload, 'row', axis=0, tiled=False)  79.5 us
    all_gather x1, waiting for transfers between devices, on_device(): second_all = lax.all_gather(second_payload, 'row', axis=0, tiled=False)  78.3 us
    select_n x1, other arithmetic, selected_columns(): chosen = jnp.where(hit[:, None, None], pieces[:, :, p, :], chosen)  20.9 us
    another operation x1, other arithmetic, selected_columns(): stacked = jnp.stack(outs, axis=2)  20 us
  transfers between devices with their start and end apart: 3, of which 3 were waited for; matrix products, arithmetic and copies ran while one was open for 4% of the time, Pallas kernels for 0%

profile of v1, /device:TPU:6, one launch (start us, length us, event | category | flops | bytes accessed | tf_op | source)
XLA Modules:
  0.0 449.7 jit_solution(17765461520942548366)
XLA Ops:
  6.5 0.7 convert_bitcast_fusion.1
  7.2 1.5 fusion.20
  8.7 0.0 all-gather.7.cloned.1.call-update
  8.7 0.0 all-gather.9.cloned.1.call-start
  8.7 0.7 all-gather.9.cloned.1.call-update
  9.4 0.0 all-gather.11.cloned.1.call-start
  9.5 1.3 fusion.27
  10.8 1.4 fusion.26
  12.2 0.7 convert_bitcast_fusion
  12.9 79.5 %all-gather.7.cloned.1.call-done = bf16[2304,256]{1,0:T(8,128)(2,1)} async-done(((bf16[144,256]{1,0:T(8,128)(2,1)}), bf16[2304,256]{1,0:T(8,128)(2,1)}) %all-gather.7.cloned.1.call-update) | async-done | bytes 1179664 | tf_op jit(solution)/shard_map/all_gather | solution.py:60
  92.3 0.8 slice.158
  93.1 0.1 copy.12
  93.2 2.8 slice_convert_fusion.1
  96.0 2.3 reshape.375
  98.3 2.2 fusion.25
  100.6 0.6 copy.6
  101.2 0.6 copy.7
  101.8 0.1 iota_compare_fusion.3
  101.9 1.6 add_convert_fusion.1
  103.5 2.8 convert_element_type.87
  106.3 174.6 %all-gather.9.cloned.1.call-done = bf16[9216,256]{1,0:T(8,128)(2,1)} async-done(((bf16[144,256]{1,0:T(8,128)(2,1)}), bf16[9216,256]{1,0:T(8,128)(2,1)}) %all-gather.9.cloned.1.call-update) | async-done | bytes 4718608 | tf_op jit(solution)/shard_map/all_gather | solution.py:61
  281.0 0.9 slice.162
  281.9 4.7 %slice.163 = bf16[64,128,256]{2,1,0:T(8,128)(2,1)} slice(bf16[64,144,256]{2,1,0:T(8,128)(2,1)} %bitcast.89), slice={[0:64], [0:128], [0:256]} | slice | bytes 8388608 | tf_op jit(solution)/shard_map/slice | solution.py:18
  286.6 0.1 copy.13
  286.7 6.9 %reshape.369 = bf16[64,128,2,128]{3,2,1,0:T(2,128)(2,1)} reshape(bf16[64,128,256]{2,1,0:T(8,128)(2,1)} %slice.163) | data formatting | bytes 8388608 | tf_op jit(solution)/shard_map/reshape | solution.py:39
  293.6 2.7 compare_bitcast_fusion.2
  296.3 20.9 %broadcast_select_fusion.1 = (bf16[64,128,1,128]{3,2,1,0:T(2,128)(2,1)S(1)}, bf16[64,128,1,128]{3,2,1,0:T(2,128)(2,1)S(1)}, bf16[64,128,1,128]{3,2,1,0:T(2,128)(2,1)S(1)}, bf16[64,128,1,128]{3,2,1,0:T(2,128)(2,1)S(1)}) fusion(pred[64]{0:T(512)(128)(4,1)S(1)} %get-tuple-element.46, pred[64]{0:T(512)(128)(4,1)S(1)} %get-tuple-element.39, ...), kind=kLoop, calls=%fused_computation.1 | loop fusion | flops 8388608 | bytes 12583424 | tf_op jit(solution)/shard_map/jit(_where)/select_n | solution.py:45
  317.2 0.0 copy-start
  317.2 20.0 %pad_maximum_fusion = (bf16[64,128,2,128]{3,2,1,0:T(2,128)(2,1)S(1)}, bf16[64,128,2,128]{3,2,1,0:T(2,128)(2,1)}) fusion(bf16[64,128,1,128]{3,2,1,0:T(2,128)(2,1)S(1)} %get-tuple-element.32, bf16[64,128,1,128]{3,2,1,0:T(2,128)(2,1)S(1)} %get-tuple-element.31, bf16[64,128,1,128]{3,2,1,0:T(2,128)(2,1)S(1)} %get-tuple-element.30, ...), kind=kLoop, calls=%fused_computation.14 | loop fusion | flops 16777216 | bytes 16777216 | tf_op jit(solution)/shard_map/stack | solution.py:47
  337.2 0.7 fusion.15
  338.0 0.6 fusion.21
  338.6 0.0 all-gather.11.cloned.1.call-update
  344.0 0.1 reshape.378
  344.1 0.1 fusion.22
  344.2 0.1 maximum_multiply_fusion
  344.4 78.3 %all-gather.11.cloned.1.call-done = bf16[2304,256]{1,0:T(8,128)(2,1)} async-done(((bf16[144,256]{1,0:T(8,128)(2,1)}), bf16[2304,256]{1,0:T(8,128)(2,1)}) %all-gather.11.cloned.1.call-update) | async-done | bytes 1179664 | tf_op jit(solution)/shard_map/all_gather | solution.py:71
  422.7 2.8 slice_convert_fusion
  425.5 0.8 slice.168
  426.3 2.5 reshape.380
  428.7 2.2 fusion.24
  431.0 0.6 copy.10
  431.6 1.6 copy.11
  433.2 0.1 copy.14
  433.3 0.1 iota_compare_fusion.1
  433.4 0.1 iota_compare_fusion.2
  433.4 2.7 add_convert_fusion
  436.2 2.8 convert_element_type.98
  439.0 4.2 fusion.12
  (7 shorter events, 0.0 us)
Async XLA Ops:
  6.5 85.8 %all-gather.7.cloned.1.call-start = ((), (), s32[]{:S(2)}) async-start(), calls=%async_computation | async-start | bytes 1253376 | tf_op jit(solution)/shard_map/all_gather | solution.py:60
  8.7 272.3 %all-gather.9.cloned.1.call-start = ((), (), s32[]{:S(2)}) async-start(), calls=%async_computation.1 | async-start | bytes 4792320 | tf_op jit(solution)/shard_map/all_gather | solution.py:61
  9.4 413.2 %all-gather.11.cloned.1.call-start = ((), (), s32[]{:S(2)}) async-start(), calls=%async_computation.2 | async-start | bytes 1253376 | tf_op jit(solution)/shard_map/all_gather | solution.py:71
  317.2 20.0 %copy-start = (bf16[128,8192]{1,0:T(8,128)(2,1)S(1)}, bf16[128,8192]{1,0:T(8,128)(2,1)}, u32[]{:S(2)}) copy-start(bf16[128,8192]{1,0:T(8,128)(2,1)} %convert_element_type.87) | copy-start | bytes 6291460
Sparse Core Ops, SparseCore 0:
  10.0 82.3 all-gather.6
  95.0 185.8 all-gather.8
  338.7 83.8 all-gather.10
